TPU v7x, 512 devices: a whole 4x4x16 slice. The times are simulated.
512 devices in a mesh: row: 16 (over x, y), col: 32 (over z, core).
Axes of the slice: x: 4, y: 4, z: 16, core: 2. Of those that a mesh axis runs over, the one named last changes fastest.
Arguments:
- hidden: bfloat16 [2560, 7168], P('col', 'row'), may hold values from -6 to 6
- ln_gain: bfloat16 [7168], P('row'), may hold values from 0.099609375 to 1.8984375
- ln_shift: bfloat16 [7168], P('row'), may hold values from -3 to 3
- qkv_weight: bfloat16 [7168, 12288], P('row', 'col'), may hold values from -0.0625 to 0.0625
- qkv_bias: bfloat16 [12288], P('col'), may hold values from -5.351432 to 5.351432
- out_weight: bfloat16 [4096, 7168], P('row', 'col'), may hold values from -0.09375 to 0.09375
- out_bias: bfloat16 [7168], P('col'), may hold values from -3 to 3
- down_qkv: bfloat16 [64, 7168, 16], P(None, 'row'), may hold values from -0.0625 to 0.0625
- up_qkv: bfloat16 [64, 16, 12288], P(None, None, 'col'), may hold values from -1.5 to 1.5
- down_out: bfloat16 [64, 16, 4096], P(None, None, 'col'), may hold values from -0.09375 to 0.09375
- up_out: bfloat16 [64, 16, 7168], P(None, None, 'col'), may hold values from -1.5 to 1.5
- prompt_lens: int32 [16], replicated, may hold values from 1 to 80, as said below
- suffix_lens: int32 [16, 16], replicated, may hold values from 1 to 5, as said below
- group_sizes: int32 [16], replicated, may hold values from 8 to 16, as said below
- group_adapter_choice: int32 [16], replicated, may hold values from 0 to 15
- chosen: int32 [16], replicated, may hold values from 0 to 63, as said below
Outputs:
- attn_out: bfloat16 [2560, 7168], P('row', 'col')
Inputs may be any that keep to these rules, and one draw needn't show every extreme that they name: `prompt_lens`: one group, drawn from the seed, has a prompt of exactly 80 tokens, 16 requests and every suffix 5 long, so it fills all 160 slots. `suffix_lens`: entries past a group's number of requests are not used. `group_sizes`: A group's prompt and its live suffixes take at most 160 slots. `chosen`: 16 different bank indices.
All inputs are finite; a program needn't handle non-finite values.
Results may differ from a plain program's by a relative error of at most 0.012.
The roundings to bfloat16 on the way count: a program that leaves them out, or rounds other values in their place, can miss the bound.
Values may be sent and summed in bfloat16 or wider, within the bound.
No kernel may reach another device: no remote copies, remote signals or barrier semaphores. Data moves between devices by JAX's collectives and lax.ppermute only.
A program may use at most 64 MiB of HBM per device.

v0:
```python
import jax
import jax.numpy as jnp
from jax import lax
from jax.sharding import PartitionSpec as P

HEAD_SIZE = 128
GCAP = 160
WIN = 53


def broadcast(x, axis, root):
    mine = lax.axis_index(axis) == root
    return lax.psum(jnp.where(mine, x, jnp.zeros_like(x)), axis)


def group_layout(prompt, count, suffix):
    offsets = jnp.arange(GCAP, dtype=jnp.int32)
    chosen_adapter_index = jnp.arange(suffix.shape[0], dtype=jnp.int32)
    live_lens = jnp.where(chosen_adapter_index < count, suffix, 0)
    end_at = prompt + jnp.cumsum(live_lens)
    group_start_rows = end_at - live_lens
    request = jnp.sum((offsets[:, None] >= end_at[None, :]).astype(jnp.int32), axis=1)
    in_prompt = offsets < prompt
    live_rows = in_prompt | (request < count)
    group_begin_row = jnp.sum(
        jnp.where(chosen_adapter_index[None, :] == request[:, None], group_start_rows[None, :], 0),
        axis=1,
    )
    position = jnp.where(in_prompt, offsets, prompt + offsets - group_begin_row)
    request_of = jnp.where(in_prompt, -1, request)
    return (live_rows, request_of, position)


def key_mask(live_rows, request_of, position):
    shared = (request_of[None, :] == -1) | (request_of[None, :] == request_of[:, None])
    causal = position[None, :] <= position[:, None]
    within = (position[:, None] - position[None, :] < WIN) | (position[None, :] == 0)
    allowed = live_rows[:, None] & live_rows[None, :] & shared & causal & within
    first_key = jnp.arange(GCAP)[None, :] == 0
    return jnp.where(live_rows[:, None], allowed, first_key)


def attention(queries, key_rows, value_rows, allowed):
    scores = jnp.einsum("qhe,khe->hqk", queries, key_rows, preferred_element_type=jnp.float32)
    scores = jnp.where(allowed[None], scores, -1e30)
    highest = jnp.max(scores, axis=2, keepdims=True)
    weights = jnp.where(allowed[None], jnp.exp(scores - highest), 0.0)
    probs = (weights / jnp.sum(weights, axis=2, keepdims=True)).astype(jnp.bfloat16)
    mixed_rows = jnp.einsum("hqk,khe->qhe", probs, value_rows, preferred_element_type=jnp.float32)
    return mixed_rows.astype(jnp.bfloat16).reshape(queries.shape[0], -1)


def local(
    hidden,
    ln_gain,
    ln_shift,
    qkv_weight,
    qkv_bias,
    out_weight,
    out_bias,
    down_qkv,
    up_qkv,
    down_out,
    up_out,
    prompt_lens,
    suffix_lens,
    group_sizes,
    group_adapter_choice,
    chosen,
):
    row_index = lax.axis_index("row")
    row_count = lax.axis_size("row")
    adapters = chosen[group_adapter_choice]
    own_adapter = adapters[row_index]
    low_rank = down_qkv.shape[2]
    features, gain_full, shift_full = (
        lax.all_gather(hidden, "row", axis=1, tiled=True),
        lax.all_gather(ln_gain, "row", axis=0, tiled=True),
        lax.all_gather(ln_shift, "row", axis=0, tiled=True),
    )
    widened = features.astype(jnp.float32)
    average = jnp.mean(widened, axis=1, keepdims=True)
    centred = widened - average
    spread = jnp.mean(centred * centred, axis=1, keepdims=True)
    normed = (
        centred * lax.rsqrt(spread + 1e-05) * gain_full.astype(jnp.float32)
        + shift_full.astype(jnp.float32)
    ).astype(jnp.bfloat16)
    per_group = lax.axis_size("col") // row_count
    received = []
    for offset in range(per_group):
        received.append(broadcast(normed, "col", row_index * per_group + offset))
    group_rows = jnp.concatenate(received, axis=0)
    lowered = jnp.transpose(down_qkv[adapters], (1, 0, 2)).reshape(
        down_qkv.shape[1], row_count * low_rank
    )
    sliced = group_rows
    own_down = lax.dynamic_slice_in_dim(
        lax.all_gather(lowered, "row", axis=0, tiled=True), row_index * low_rank, low_rank, 1
    )
    projected = jnp.dot(
        sliced,
        lax.all_gather(qkv_weight, "row", axis=0, tiled=True),
        preferred_element_type=jnp.float32,
    )
    reduced = jnp.dot(sliced, own_down, preferred_element_type=jnp.float32)
    projected = (
        projected
        + qkv_bias.astype(jnp.float32)
        + jnp.dot(
            reduced.astype(jnp.bfloat16), up_qkv[own_adapter], preferred_element_type=jnp.float32
        )
    )
    heads_here = projected.shape[1] // (3 * HEAD_SIZE)
    shaped = projected.reshape(GCAP, heads_here, 3, HEAD_SIZE)
    queries = (shaped[:, :, 0] * HEAD_SIZE ** (-0.5)).astype(jnp.bfloat16)
    key_rows = shaped[:, :, 1].astype(jnp.bfloat16)
    value_rows = shaped[:, :, 2].astype(jnp.bfloat16)
    live_rows, request_of, position = group_layout(
        prompt_lens[row_index], group_sizes[row_index], suffix_lens[row_index]
    )
    mixed_rows = attention(queries, key_rows, value_rows, key_mask(live_rows, request_of, position))
    down_here = down_out[own_adapter]
    all_heads, down_full = (
        lax.all_gather(mixed_rows, "col", axis=1, tiled=True),
        lax.all_gather(down_here, "col", axis=1, tiled=True),
    )
    reduced_out = lax.dot_general(
        all_heads, down_full, (((1,), (1,)), ((), ())), preferred_element_type=jnp.float32
    ).astype(jnp.bfloat16)
    sliced = all_heads
    combined = jnp.dot(
        sliced,
        lax.all_gather(out_weight, "row", axis=0, tiled=True),
        preferred_element_type=jnp.float32,
    )
    result = (
        combined
        + out_bias.astype(jnp.float32)
        + jnp.dot(reduced_out, up_out[own_adapter], preferred_element_type=jnp.float32)
    )
    return (result * live_rows[:, None].astype(jnp.float32)).astype(jnp.bfloat16)


def solution(mesh):
    in_specs = (
        P("col", "row"),
        P("row"),
        P("row"),
        P("row", "col"),
        P("col"),
        P("row", "col"),
        P("col"),
        P(None, "row", None),
        P(None, None, "col"),
        P(None, None, "col"),
        P(None, None, "col"),
        P(),
        P(),
        P(),
        P(),
        P(),
    )
    out_specs = P("row", "col")
    return jax.shard_map(local, mesh=mesh, in_specs=in_specs, out_specs=out_specs, check_vma=False)
```

profile of v0, /device:TPU:2, one launch (start us, length us, event | category | flops | bytes accessed | tf_op | source)
XLA Modules:
  0.0 603.2 jit_solution(5477577475409524125)
XLA Ops:
  6.5 0.7 all-gather.17.cloned.1.call-update
  7.3 1.3 dynamic-slice
  9.3 0.9 dynamic-update-slice
  10.1 0.9 dynamic-update-slice.1
  11.0 69.1 %all-reduce.3 = (bf16[7168]{0:T(1024)(128)(2,1)S(1)}, bf16[7168]{0:T(1024)(128)(2,1)S(1)}) all-reduce(bf16[7168]{0:T(1024)(128)(2,1)S(1)} %dynamic-update-slice, bf16[7168]{0:T(1024)(128)(2,1)S(1)} %dynamic-update-slice.1), channel_id=1, replica_groups=mesh['row'=16,'col'=32] {'row'}, use_global_device_ids=true, to_apply=%add | all-reduce | flops 14336 | bytes 57344
  80.2 3.6 copy.26
  83.7 2.4 reshape.225
  86.2 1.6 convert_reduce_fusion
  88.2 1.6 broadcast_select_fusion
  89.8 1.2 broadcast_select_fusion.1
  91.1 0.7 all-gather.9.cloned.1.call-update
  91.8 0.7 gather_fusion
  93.1 0.8 copy.27
  96.6 1.3 compare_select_fusion.3
  98.0 0.6 dynamic_slice.27
  99.3 0.7 add_reduce_fusion
  100.2 1.3 fusion.54
  102.2 1.3 fusion.57
  103.5 209.5 %all-reduce.6.cloned.1.call-done = (bf16[80,7168]{1,0:T(8,128)(2,1)}, bf16[80,7168]{1,0:T(8,128)(2,1)}) async-done(((bf16[80,7168]{1,0:T(8,128)(2,1)}, bf16[80,7168]{1,0:T(8,128)(2,1)}), (bf16[80,7168]{1,0:T(8,128)(2,1)}, bf16[80,7168]{1,0:T(8,128)(2,1)})) %all-reduce.6.cloned.1.call-update) | async-done | bytes 2293776 | tf_op jit(solution)/shard_map/psum | solution.py:13
  313.0 1.4 constant_dynamic-update-slice_fusion.1
  314.7 74.3 %all-gather.9.cloned.1.call-done = bf16[7168,384]{1,0:T(8,128)(2,1)} async-done(((bf16[448,384]{1,0:T(8,128)(2,1)}), bf16[7168,384]{1,0:T(8,128)(2,1)}) %all-gather.9.cloned.1.call-update) | async-done | bytes 5505040 | tf_op jit(solution)/shard_map/all_gather | solution.py:103
  388.9 4.6 convolution_add_fusion.1
  393.6 62.4 %all-gather.11.cloned.1.call-done = bf16[7168,256]{1,0:T(8,128)(2,1)} async-done(((bf16[448,256]{1,0:T(8,128)(2,1)}), bf16[7168,256]{1,0:T(8,128)(2,1)}) %all-gather.11.cloned.1.call-update) | async-done | bytes 3670032 | tf_op jit(solution)/shard_map/all_gather | solution.py:99
  455.9 4.1 convolution_add_fusion
  460.0 1.1 reshape.192
  461.9 1.0 fusion.19
  463.5 0.7 constant_dynamic-slice_fusion
  464.2 31.3 %all-gather.1 = bf16[1,16,4096]{2,1,0:T(8,128)(2,1)S(1)} all-gather(bf16[1,16,128]{2,1,0:T(8,128)(2,1)S(1)} %constant_dynamic-slice_fusion), channel_id=3, replica_groups=mesh['row'=16,'col'=32] {'col'}, dimensions={2}, use_global_device_ids=true | all-gather | bytes 135168 | tf_op jit(solution)/shard_map/all_gather | solution.py:126
  495.5 37.9 %all-gather.15.cloned.1.call-done = bf16[160,1,4096]{2,0,1:T(8,128)(2,1)} async-done(((bf16[160,1,128]{2,0,1:T(8,128)(2,1)}), bf16[160,1,4096]{2,0,1:T(8,128)(2,1)}) %all-gather.15.cloned.1.call-update) | async-done | bytes 1310736 | tf_op jit(solution)/shard_map/all_gather | solution.py:125
  533.4 2.0 fusion.27
  535.5 57.6 %all-gather.13.cloned.1.call-done = bf16[4096,224]{0,1:T(8,128)(2,1)} async-done(((bf16[256,224]{0,1:T(8,128)(2,1)}), bf16[4096,224]{0,1:T(8,128)(2,1)}) %all-gather.13.cloned.1.call-update) | async-done | bytes 1835024 | tf_op jit(solution)/shard_map/all_gather | solution.py:134
  593.1 3.3 fusion.16
  (55 shorter events, 5.0 us)
Async XLA Ops:
  6.5 86.0 %copy-start = (bf16[64,448,16]{1,2,0:T(8,128)(2,1)S(1)}, bf16[64,448,16]{1,2,0:T(8,128)(2,1)}, u32[]{:S(2)}) copy-start(bf16[64,448,16]{1,2,0:T(8,128)(2,1)} %param.23) | copy-start | bytes 2752516
  6.5 73.6 %all-gather.17.cloned.1.call-start = ((), (), s32[]{:S(2)}) async-start(), calls=%async_computation.4 | async-start | bytes 1392640 | tf_op jit(solution)/shard_map/all_gather | solution.py:77
  7.3 305.7 %all-reduce.6.cloned.1.call-start = ((), (), s32[]{:S(2)}) async-start(), calls=%async_computation.5 | async-start | bytes 4587520 | tf_op jit(solution)/shard_map/psum | solution.py:13
  89.8 2.0 copy-start.4
  89.8 2.0 copy-start.1
  91.0 297.9 %all-gather.9.cloned.1.call-start = ((), (), s32[]{:S(2)}) async-start(), calls=%async_computation | async-start | bytes 5849088 | tf_op jit(solution)/shard_map/all_gather | solution.py:103
  91.7 364.2 %all-gather.11.cloned.1.call-start = ((), (), s32[]{:S(2)}) async-start(), calls=%async_computation.1 | async-start | bytes 3899392 | tf_op jit(solution)/shard_map/all_gather | solution.py:99
  92.5 1.5 copy-start.3
  92.5 3.4 copy-start.5
  92.5 5.5 copy-start.6
  94.0 439.5 %all-gather.15.cloned.1.call-start = ((), (), s32[]{:S(2)}) async-start(), calls=%async_computation.3 | async-start | bytes 1351680 | tf_op jit(solution)/shard_map/all_gather | solution.py:125
  313.0 1.6 copy-start.2
  460.0 3.4 copy-start.7
  462.9 130.2 %all-gather.13.cloned.1.call-start = ((), (), s32[]{:S(2)}) async-start(), calls=%async_computation.2 | async-start | bytes 1949696 | tf_op jit(solution)/shard_map/all_gather | solution.py:134
Sparse Core Ops, SparseCore 0:
  10.4 62.7 all-gather.16
  91.1 221.7 all-reduce.5
  316.0 72.8 all-gather.8
  391.8 64.0 all-gather.10
  463.0 70.3 all-gather.14
  536.3 56.7 all-gather.12
where the time goes:
time: 604 us; the launch traced here: 603 us
  waiting for transfers between devices  444 us (74%)
  blocking collectives  100 us (17%)
  local copies, waits for them, and re-layouts  16.6 us (3%)
  between operations  16.3 us (3%)
  matrix products  15.3 us (3%)
  other arithmetic  10.7 us (2%)
    psum x1, waiting for transfers between devices, broadcast(): return lax.psum(jnp.where(mine, x, jnp.zeros_like(x)), axis)  209 us
    all_gather x1, waiting for transfers between devices, local(): lax.all_gather(qkv_weight, 'row', axis=0, tiled=True)  74.3 us
    unnamed x1, blocking collectives  69.1 us
    all_gather x1, waiting for transfers between devices, local(): lax.all_gather(lowered, 'row', axis=0, tiled=True)  62.4 us
    all_gather x1, waiting for transfers between devices, local(): lax.all_gather(out_weight, 'row', axis=0, tiled=True)  57.6 us
    all_gather x1, waiting for transfers between devices, local(): lax.all_gather(mixed_rows, 'col', axis=1, tiled=True)  37.9 us
    all_gather x1, blocking collectives, local(): lax.all_gather(down_here, 'col', axis=1, tiled=True)  31.3 us
  transfers between devices with their start and end apart: 6, of which 5 were waited for; matrix products, arithmetic and copies ran while one was open for 4% of the time, Pallas kernels for 0%

commit v1 on v0

--- a/solution.py
+++ b/solution.py
@@ -6,6 +6,12 @@
 HEAD_SIZE = 128
 GCAP = 160
 WIN = 53
+
+
+def gather_by_exchange(x, axis, dim):
+    size = lax.axis_size(axis)
+    repeats = [size if d == dim else 1 for d in range(x.ndim)]
+    return lax.all_to_all(jnp.tile(x, repeats), axis, split_axis=dim, concat_axis=dim, tiled=True)
 
 
 def broadcast(x, axis, root):
@@ -122,7 +128,7 @@
     mixed_rows = attention(queries, key_rows, value_rows, key_mask(live_rows, request_of, position))
     down_here = down_out[own_adapter]
     all_heads, down_full = (
-        lax.all_gather(mixed_rows, "col", axis=1, tiled=True),
+        gather_by_exchange(mixed_rows, "col", 1),
         lax.all_gather(down_here, "col", axis=1, tiled=True),
     )
     reduced_out = lax.dot_general(

time: 604 us -> 573 us (0.949)
  the two profiles are of different devices: /device:TPU:2 before, /device:TPU:1 now
where the time goes in v1:
time: 573 us; the launch traced here: 572 us
  waiting for transfers between devices  357 us (62%)
  blocking collectives  144 us (25%)
  local copies, waits for them, and re-layouts  17.8 us (3%)
  between operations  16 us (3%)
  matrix products  13.7 us (2%)
  starting transfers between devices  13.6 us (2%)
  other arithmetic  10.5 us (2%)
    psum x1, waiting for transfers between devices, broadcast(): return lax.psum(jnp.where(mine, x, jnp.zeros_like(x)), axis)  217 us
    all_gather x1, blocking collectives, local(): lax.all_gather(down_here, 'col', axis=1, tiled=True)  82.3 us
    all_gather x1, waiting for transfers between devices, local(): lax.all_gather(qkv_weight, 'row', axis=0, tiled=True)  75.2 us
    all_gather x1, waiting for transfers between devices, local(): lax.all_gather(lowered, 'row', axis=0, tiled=True)  62.6 us
    unnamed x1, blocking collectives  61.8 us
    all_to_all x1, starting transfers between devices, gather_by_exchange(): lax.all_to_all(jnp.tile(x, repeats), axis, split_axis=dim, concat_axis=di...  13.5 us
  transfers between devices with their start and end apart: 6, of which 3 were waited for; matrix products, arithmetic and copies ran while one was open for 4% of the time, Pallas kernels for 0%

profile of v1, /device:TPU:1, one launch (start us, length us, event | category | flops | bytes accessed | tf_op | source)
XLA Modules:
  0.0 572.4 jit_solution(7231011913092822895)
XLA Ops:
  6.5 0.7 all-gather.13.cloned.1.call-update
  7.3 1.3 dynamic-slice
  9.3 0.9 dynamic-update-slice
  10.1 0.9 dynamic-update-slice.1
  11.0 61.8 %all-reduce.3 = (bf16[7168]{0:T(1024)(128)(2,1)S(1)}, bf16[7168]{0:T(1024)(128)(2,1)S(1)}) all-reduce(bf16[7168]{0:T(1024)(128)(2,1)S(1)} %dynamic-update-slice, bf16[7168]{0:T(1024)(128)(2,1)S(1)} %dynamic-update-slice.1), channel_id=1, replica_groups=mesh['row'=16,'col'=32] {'row'}, use_global_device_ids=true, to_apply=%add | all-reduce | flops 14336 | bytes 57344
  72.9 3.6 copy.27
  76.5 2.4 reshape.227
  78.9 1.6 convert_reduce_fusion
  80.9 1.6 broadcast_select_fusion
  82.5 1.2 broadcast_select_fusion.1
  83.7 0.7 all-gather.7.cloned.1.call-update
  84.5 0.7 gather_fusion
  85.8 0.8 copy.28
  89.2 1.3 compare_select_fusion.3
  90.6 0.6 dynamic_slice.27
  91.8 0.7 add_reduce_fusion
  92.7 1.3 fusion.56
  94.0 0.6 broadcast_compare_fusion
  94.7 1.2 fusion.59
  95.9 216.8 %all-reduce.6.cloned.1.call-done = (bf16[80,7168]{1,0:T(8,128)(2,1)}, bf16[80,7168]{1,0:T(8,128)(2,1)}) async-done(((bf16[80,7168]{1,0:T(8,128)(2,1)}, bf16[80,7168]{1,0:T(8,128)(2,1)}), (bf16[80,7168]{1,0:T(8,128)(2,1)}, bf16[80,7168]{1,0:T(8,128)(2,1)})) %all-reduce.6.cloned.1.call-update) | async-done | bytes 2293776 | tf_op jit(solution)/shard_map/psum | solution.py:19
  312.7 1.4 constant_dynamic-update-slice_fusion.1
  314.4 75.2 %all-gather.7.cloned.1.call-done = bf16[7168,384]{1,0:T(8,128)(2,1)} async-done(((bf16[448,384]{1,0:T(8,128)(2,1)}), bf16[7168,384]{1,0:T(8,128)(2,1)}) %all-gather.7.cloned.1.call-update) | async-done | bytes 5505040 | tf_op jit(solution)/shard_map/all_gather | solution.py:109
  389.6 4.6 convolution_add_fusion.1
  394.2 62.6 %all-gather.9.cloned.1.call-done = bf16[7168,256]{1,0:T(8,128)(2,1)} async-done(((bf16[448,256]{1,0:T(8,128)(2,1)}), bf16[7168,256]{1,0:T(8,128)(2,1)}) %all-gather.9.cloned.1.call-update) | async-done | bytes 3670032 | tf_op jit(solution)/shard_map/all_gather | solution.py:105
  456.8 4.1 convolution_add_fusion
  461.0 1.0 reshape.196
  463.2 1.2 tile.9
  464.4 13.5 %all-to-all-start = ((bf16[160,32,128]{2,0,1:T(8,128)(2,1)}), bf16[160,32,128]{2,0,1:T(8,128)(2,1)S(1)}, u32[]{:S(2)}, u32[]{:S(2)}) async-start(bf16[160,32,128]{2,0,1:T(8,128)(2,1)} %tile.9), calls=%async_computation | async-start | bytes 2621440 | tf_op jit(solution)/shard_map/all_to_all | solution.py:14
  478.5 0.7 constant_dynamic-slice_fusion
  479.2 82.3 %all-gather = bf16[1,16,4096]{2,1,0:T(8,128)(2,1)S(1)} all-gather(bf16[1,16,128]{2,1,0:T(8,128)(2,1)S(1)} %constant_dynamic-slice_fusion), channel_id=2, replica_groups=mesh['row'=16,'col'=32] {'col'}, dimensions={2}, use_global_device_ids=true | all-gather | bytes 135168 | tf_op jit(solution)/shard_map/all_gather | solution.py:132
  561.5 1.4 fusion.29
  562.9 2.9 fusion.18
  (55 shorter events, 4.7 us)
Async XLA Ops:
  6.5 78.7 %copy-start = (bf16[64,448,16]{1,2,0:T(8,128)(2,1)S(1)}, bf16[64,448,16]{1,2,0:T(8,128)(2,1)}, u32[]{:S(2)}) copy-start(bf16[64,448,16]{1,2,0:T(8,128)(2,1)} %param.23) | copy-start | bytes 2752516
  6.5 66.3 %all-gather.13.cloned.1.call-start = ((), (), s32[]{:S(2)}) async-start(), calls=%async_computation.4 | async-start | bytes 1392640 | tf_op jit(solution)/shard_map/all_gather | solution.py:83
  7.3 305.5 %all-reduce.6.cloned.1.call-start = ((), (), s32[]{:S(2)}) async-start(), calls=%async_computation.5 | async-start | bytes 4587520 | tf_op jit(solution)/shard_map/psum | solution.py:19
  83.7 0.8 copy-start.4
  83.7 0.8 copy-start.1
  83.7 305.9 %all-gather.7.cloned.1.call-start = ((), (), s32[]{:S(2)}) async-start(), calls=%async_computation.1 | async-start | bytes 5849088 | tf_op jit(solution)/shard_map/all_gather | solution.py:109
  84.4 372.4 %all-gather.9.cloned.1.call-start = ((), (), s32[]{:S(2)}) async-start(), calls=%async_computation.2 | async-start | bytes 3899392 | tf_op jit(solution)/shard_map/all_gather | solution.py:105
  85.2 1.5 copy-start.3
  85.2 3.4 copy-start.5
  85.2 5.3 copy-start.6
  312.7 1.6 copy-start.2
  463.2 15.3 %copy-start.7 = (bf16[224]{0:T(256)(128)(2,1)S(1)}, bf16[224]{0:T(256)(128)(2,1)}, u32[]{:S(2)}) copy-start(bf16[224]{0:T(256)(128)(2,1)} %param.22) | copy-start | bytes 1348
  464.4 97.1 %all-to-all-start = ((bf16[160,32,128]{2,0,1:T(8,128)(2,1)}), bf16[160,32,128]{2,0,1:T(8,128)(2,1)S(1)}, u32[]{:S(2)}, u32[]{:S(2)}) async-start(bf16[160,32,128]{2,0,1:T(8,128)(2,1)} %tile.9), calls=%async_computation | async-start | bytes 2621440 | tf_op jit(solution)/shard_map/all_to_all | solution.py:14
  477.9 85.0 %all-gather.11.cloned.1.call-start = ((), (), s32[]{:S(2)}) async-start(), calls=%async_computation.3 | async-start | bytes 1949696 | tf_op jit(solution)/shard_map/all_gather | solution.py:140
Sparse Core Ops, SparseCore 0:
  10.4 61.9 all-gather.12
  83.8 228.8 all-reduce.5
  315.8 73.7 all-gather.6
  392.5 64.3 all-gather.8
  481.4 58.0 all-gather.10
